TPU v7x, 512 devices: a whole 4x4x16 slice. The times are simulated.
512 devices in a mesh: grp: 2 (over core), dp: 32 (over x_hi, z), seq: 8 (over y, x_lo).
Axes of the slice: x: 4 (x_hi: 2, x_lo: 2; x = x_hi * 2 + x_lo), y: 4, z: 16, core: 2. Of those that a mesh axis runs over, the one named last changes fastest.
Arguments:
- latents: float32 [64, 256, 2432], P(('grp', 'dp'), None, 'seq'), may hold values from -6 to 6
- step_noise: bfloat16 [2, 64, 256, 2432], P(None, ('grp', 'dp'), None, 'seq'), may hold values from -6 to 6
- ada_table: float32 [10, 2, 2432], replicated
- qkv_weight: bfloat16 [3, 2048, 2432], P(None, 'seq', ('grp', 'dp')), may hold values from -0.125 to 0.125
- out_weight: bfloat16 [2048, 2432], P(('grp', 'dp'), 'seq'), may hold values from -0.125 to 0.125
- rewards: float32 [64], replicated, may hold values from -4 to 4
- group_ids: int32 [64], replicated, may hold values from 0 to 7, as said below
- time_index: int32 [64], P(('grp', 'dp')), may hold values from 1 to 8
- log_ratio: float32 [2, 64], replicated, may hold values from -0.4 to 0.4
Outputs:
- final_latents: float32 [64, 256, 2432], P(('grp', 'dp'), None, 'seq')
- policy_loss: float32 [], replicated
- out_grad: float32 [2048, 2432], P(('grp', 'dp'), 'seq')
Inputs may be any that keep to these rules, and one draw needn't show every extreme that they name: `group_ids`: each group number names exactly 8 samples.
All inputs are finite; a program needn't handle non-finite values.
Results may differ from a plain program's by a relative error of at most 0.017.
Values may be sent and summed in bfloat16 or wider, within the bound.
No kernel may reach another device: no remote copies, remote signals or barrier semaphores. Data moves between devices by JAX's collectives and lax.ppermute only.
A program may use at most 64 MiB of HBM per device.

v0:
```python
import jax
import jax.numpy as jnp
from jax import lax
from jax.sharding import PartitionSpec as P

HD = 64
TSTEPS = 10
GSIZE = 8
SDE_NOISE = 0.7
CLIP_RANGE = 0.2
REWARD_FLOOR = 0.75
NORM_EPS = 1e-06


def advantages(rewards, group_ids):
    same_group = (group_ids[:, None] == group_ids[None, :]).astype(jnp.float32)
    centre = jnp.sum(same_group * rewards[None, :], 1) / GSIZE
    spread = jnp.sum(same_group * (rewards[None, :] - centre[:, None]) ** 2, 1) / GSIZE
    return (rewards - centre) / jnp.maximum(jnp.sqrt(spread), REWARD_FLOOR)


def policy_terms(advantage, log_ratio):
    ratios = jnp.exp(log_ratio)
    plain = ratios * advantage[None, :]
    bounded = jnp.clip(ratios, 1.0 - CLIP_RANGE, 1.0 + CLIP_RANGE) * advantage[None, :]
    count = 2.0 * advantage.shape[0]
    loss_value = -jnp.sum(jnp.minimum(plain, bounded)) / count
    coef = jnp.where(plain <= bounded, -plain / count, jnp.float32(0.0))
    return (loss_value, coef)


def on_device(
    latents,
    step_noise,
    ada_table,
    qkv_weight,
    out_weight,
    rewards,
    group_ids,
    time_index,
    log_ratio,
):
    qkv_full, out_rows = (
        lax.all_gather(qkv_weight, ("grp", "dp"), axis=2, tiled=True),
        lax.all_gather(out_weight, ("grp", "dp"), axis=0, tiled=True),
    )
    group_width = qkv_full.shape[1]
    heads_here = group_width // HD
    model_width = qkv_full.shape[2]
    projection = qkv_full.reshape(3 * group_width, model_width)
    samples = rewards.shape[0]
    seq_len = latents.shape[1]
    block_rows = min(512, seq_len)
    advantage = advantages(rewards, group_ids)
    loss_value, coef = policy_terms(advantage, log_ratio)
    my_index = lax.axis_index(("grp", "dp"))
    chooser = (jnp.arange(samples, dtype=jnp.int32) == my_index).astype(jnp.float32)
    my_coef = jnp.sum(coef * chooser[None, :], 1)
    step_size = 1.0 / TSTEPS
    state = latents[0]
    attn_list = []
    score_list = []
    plan = jnp.arange(TSTEPS, dtype=jnp.int32)
    for section in range(2):
        index_now = time_index[0] + section
        time_now = 1.0 - index_now.astype(jnp.float32) / TSTEPS
        picker = (plan == index_now).astype(jnp.float32)
        modulate = jnp.sum(picker[:, None, None] * ada_table, 0)
        whole = lax.all_gather(state, "seq", axis=1, tiled=True)
        centre = jnp.mean(whole, -1, keepdims=True)
        spread = jnp.mean((whole - centre) ** 2, -1, keepdims=True)
        normed = (
            (whole - centre) * lax.rsqrt(spread + NORM_EPS) * (1.0 + modulate[0][None, :])
            + modulate[1][None, :]
        ).astype(jnp.bfloat16)
        proj_rows = lax.dot_general(
            normed, projection, (((1,), (1,)), ((), ())), preferred_element_type=jnp.float32
        ).astype(jnp.bfloat16)
        proj_rows = proj_rows.reshape(seq_len, 3, heads_here, HD)
        key_rows = proj_rows[:, 1]
        value_rows = proj_rows[:, 2]
        query_rows = proj_rows[0:block_rows, 0]
        logits = jnp.einsum(
            "qhe,khe->hqk", query_rows, key_rows, preferred_element_type=jnp.float32
        ) * HD ** (-0.5)
        logits = logits - jnp.max(logits, -1, keepdims=True)
        weights = jnp.exp(logits)
        probs = (weights / jnp.sum(weights, -1, keepdims=True)).astype(jnp.bfloat16)
        attn_blocks = jnp.einsum(
            "hqk,khe->qhe", probs, value_rows, preferred_element_type=jnp.float32
        ).astype(jnp.bfloat16)
        attn = attn_blocks.reshape(seq_len, group_width)
        attn_all = lax.all_gather(attn, "seq", axis=1, tiled=True)
        velocity = jnp.dot(attn_all, out_rows, preferred_element_type=jnp.float32)
        noise_level = SDE_NOISE * SDE_NOISE * time_now / (1.0 - time_now)
        std_dev = jnp.sqrt(noise_level * step_size)
        drift = velocity + noise_level / (2.0 * time_now) * (state + (1.0 - time_now) * velocity)
        mean_next = state - step_size * drift
        noise_now = step_noise[section, 0].astype(jnp.float32)
        state = mean_next + std_dev * noise_now
        factor = (
            my_coef[section]
            * -step_size
            * (1.0 + noise_level * (1.0 - time_now) / (2.0 * time_now))
            / std_dev
        )
        score_list.append((factor * noise_now).astype(jnp.bfloat16))
        attn_list.append(attn_all)
    attn_both = jnp.stack(attn_list, 0)
    score_both = jnp.stack(score_list, 0)
    gradient = lax.dot_general(
        attn_both, score_both, (((0, 1), (0, 1)), ((), ())), preferred_element_type=jnp.float32
    )
    out_grad = lax.psum_scatter(gradient, ("grp", "dp"), scatter_dimension=0, tiled=True)
    return (state[None], loss_value, out_grad)


def solution(mesh):
    return jax.shard_map(
        on_device,
        mesh=mesh,
        in_specs=(
            P(("grp", "dp"), None, "seq"),
            P(None, ("grp", "dp"), None, "seq"),
            P(),
            P(None, "seq", ("grp", "dp")),
            P(("grp", "dp"), "seq"),
            P(),
            P(),
            P(("grp", "dp")),
            P(),
        ),
        out_specs=(P(("grp", "dp"), None, "seq"), P(), P(("grp", "dp"), "seq")),
        check_vma=False,
    )
```

profile of v0, /device:TPU:8, one launch (start us, length us, event | category | flops | bytes accessed | tf_op | source)
XLA Modules:
  0.0 781.1 jit_solution(5501011536457915289)
XLA Ops:
  7.2 0.0 all-gather.18.cloned.1.call-start
  7.2 0.7 all-gather.18.cloned.1.call-update
  7.9 0.0 all-gather.8.cloned.1.call-start
  7.9 1.5 copy.31
  9.4 0.0 all-gather.8.cloned.1.call-update
  9.5 0.0 all-gather.12.cloned.1.call-start
  9.5 0.7 all-gather.12.cloned.1.call-update
  10.2 0.0 all-gather.10.cloned.1.call-start
  10.9 1.2 multiply_reduce_fusion.2
  12.1 0.1 fusion.35
  12.2 67.8 %all-gather.18.cloned.1.call-done = f32[1,256,2432]{1,2,0:T(8,128)} async-done(((f32[1,256,304]{1,2,0:T(8,128)}), f32[1,256,2432]{1,2,0:T(8,128)}) %all-gather.18.cloned.1.call-update) | async-done | bytes 2490384 | tf_op jit(solution)/shard_map/all_gather | solution.py:69
  79.9 2.2 reduce_sum.108
  82.1 0.3 copy-done
  82.4 0.4 multiply_reduce_fusion.1
  82.7 155.8 %all-gather.8.cloned.1.call-done = bf16[3,256,2432]{1,0,2:T(4,128)(2,1)} async-done(((bf16[3,256,38]{1,0,2:T(4,128)(2,1)}), bf16[3,256,2432]{1,0,2:T(4,128)(2,1)}) %all-gather.8.cloned.1.call-update) | async-done | bytes 3735568 | tf_op jit(solution)/shard_map/all_gather | solution.py:44
  238.6 8.5 %copy.32 = bf16[3,256,2432]{2,1,0:T(8,128)(2,1)} copy(bf16[3,256,2432]{1,0,2:T(4,128)(2,1)} %all-gather.8.cloned.1.call-done) | data formatting | bytes 7471104 | tf_op jit(solution)/shard_map/all_gather | solution.py:44
  247.1 4.0 convolution_convert_fusion.1
  251.2 0.2 copy.33
  251.4 0.5 fusion.44
  251.9 0.3 convolution_multiply_fusion.1
  252.3 1.0 convolution_convert_fusion.3
  253.3 0.0 all-gather.14.cloned.1.call-start
  253.5 124.9 %all-gather.12.cloned.1.call-done = bf16[2048,304]{1,0:T(8,128)(2,1)} async-done(((bf16[32,304]{1,0:T(8,128)(2,1)}), bf16[2048,304]{1,0:T(8,128)(2,1)}) %all-gather.12.cloned.1.call-update) | async-done | bytes 1245200 | tf_op jit(solution)/shard_map/all_gather | solution.py:45
  378.4 43.7 %all-gather.10.cloned.1.call-done = bf16[256,2048]{0,1:T(8,128)(2,1)} async-done(((bf16[256,256]{0,1:T(8,128)(2,1)}), bf16[256,2048]{0,1:T(8,128)(2,1)}) %all-gather.10.cloned.1.call-update) | async-done | bytes 1048592 | tf_op jit(solution)/shard_map/all_gather | solution.py:93
  422.1 3.1 fusion.18
  425.3 0.0 all-gather.16.cloned.1.call-start
  425.4 0.1 fusion.34
  425.4 66.3 %all-gather.14.cloned.1.call-done = f32[256,2432]{0,1:T(8,128)} async-done(((f32[256,304]{0,1:T(8,128)}), f32[256,2432]{0,1:T(8,128)}) %all-gather.14.cloned.1.call-update) | async-done | bytes 2490384 | tf_op jit(solution)/shard_map/all_gather | solution.py:69
  491.8 2.2 reduce_sum.112
  494.0 0.3 copy-done.1
  494.2 0.4 multiply_reduce_fusion
  494.6 4.0 convolution_convert_fusion
  498.6 0.2 copy.35
  498.8 0.5 fusion.45
  499.3 0.3 convolution_multiply_fusion
  499.7 1.0 convolution_convert_fusion.2
  500.8 0.0 reduce-scatter.2.cloned.1.call-start
  501.0 0.2 fusion.32
  501.2 0.2 fusion.33
  501.4 0.7 fusion.37
  502.1 0.6 fusion.43
  504.0 0.1 fusion.31
  504.1 44.7 %all-gather.16.cloned.1.call-done = bf16[256,2048]{0,1:T(8,128)(2,1)} async-done(((bf16[256,256]{0,1:T(8,128)(2,1)}), bf16[256,2048]{0,1:T(8,128)(2,1)}) %all-gather.16.cloned.1.call-update) | async-done | bytes 1048592 | tf_op jit(solution)/shard_map/all_gather | solution.py:93
  548.8 4.2 convolution_bitcast_fusion
  553.8 0.1 copy-done.4
  553.9 0.6 copy-done.8
  554.5 2.6 fusion.22
  557.1 215.9 %reduce-scatter.2.cloned.1.call-done = f32[32,304]{1,0:T(8,128)} async-done(((f32[2048,304]{1,0:T(8,128)}), f32[32,304]{1,0:T(8,128)}) %reduce-scatter.2.cloned.1.call-update) | async-done | bytes 38928 | tf_op jit(solution)/shard_map/reduce_scatter | solution.py:114
  (28 shorter events, 0.2 us)
Async XLA Ops:
  7.2 72.8 %all-gather.18.cloned.1.call-start = ((), (), s32[]{:S(2)}) async-start(), calls=%async_computation.7 | async-start | bytes 2801664 | tf_op jit(solution)/shard_map/all_gather | solution.py:69
  7.9 230.7 %all-gather.8.cloned.1.call-start = ((), (), s32[]{:S(2)}) async-start(), calls=%async_computation.1 | async-start | bytes 5058560 | tf_op jit(solution)/shard_map/all_gather | solution.py:44
  9.5 369.0 %all-gather.12.cloned.1.call-start = ((), (), s32[]{:S(2)}) async-start(), calls=%async_computation.3 | async-start | bytes 1597440 | tf_op jit(solution)/shard_map/all_gather | solution.py:45
  10.2 411.9 %all-gather.10.cloned.1.call-start = ((), (), s32[]{:S(2)}) async-start(), calls=%async_computation.2 | async-start | bytes 1179648 | tf_op jit(solution)/shard_map/all_gather | solution.py:93
  79.9 2.5 copy-start
  252.2 169.9 %copy-start.2 = (f32[1,256,304]{1,2,0:T(8,128)S(1)}, f32[1,256,304]{1,2,0:T(8,128)}, u32[]{:S(2)}) copy-start(f32[1,256,304]{1,2,0:T(8,128)} %param.9) | copy-start | bytes 933892
  252.2 169.9 %copy-start.3 = (bf16[2,1,256,304]{2,3,1,0:T(8,128)(2,1)S(1)}, bf16[2,1,256,304]{2,3,1,0:T(8,128)(2,1)}, u32[]{:S(2)}) copy-start(bf16[2,1,256,304]{2,3,1,0:T(8,128)(2,1)} %param.10) | copy-start | bytes 933892
  253.3 238.4 %all-gather.14.cloned.1.call-start = ((), (), s32[]{:S(2)}) async-start(), calls=%async_computation.4 | async-start | bytes 2801664 | tf_op jit(solution)/shard_map/all_gather | solution.py:69
  425.3 123.5 %all-gather.16.cloned.1.call-start = ((), (), s32[]{:S(2)}) async-start(), calls=%async_computation.5 | async-start | bytes 1179648 | tf_op jit(solution)/shard_map/all_gather | solution.py:93
  491.8 2.5 copy-start.1
  499.7 1.3 copy-start.5
  499.7 1.3 copy-start.6
  499.7 1.7 copy-start.7
  499.7 49.1 %copy-start.9 = (bf16[256,2048]{0,1:T(8,128)(2,1)S(1)}, bf16[256,2048]{0,1:T(8,128)(2,1)}, u32[]{:S(2)}) copy-start(bf16[256,2048]{0,1:T(8,128)(2,1)} %all-gather.10.cloned.1.call-done) | copy-start | bytes 3145732
  500.8 272.3 %reduce-scatter.2.cloned.1.call-start = ((), (), s32[]{:S(2)}) async-start(), calls=%async_computation.6 | async-start | bytes 3194880 | tf_op jit(solution)/shard_map/reduce_scatter | solution.py:114
  553.0 1.0 copy-start.4
  553.0 1.5 copy-start.8
Sparse Core Ops, SparseCore 0:
  10.1 69.8 all-gather.17
  83.7 154.8 all-gather.7
  241.9 136.5 all-gather.11
  380.9 41.1 all-gather.9
  425.4 66.2 all-gather.13
  500.9 47.8 all-gather.15
  554.1 218.9 reduce-scatter.1
where the time goes:
time: 782 us; the launch traced here: 781 us
  waiting for transfers between devices  721 us (92%)
  matrix products  21.8 us (3%)
  between operations  18.5 us (2%)
  local copies, waits for them, and re-layouts  12.2 us (2%)
    reduce_scatter x1, waiting for transfers between devices, on_device(): lax.psum_scatter(gradient, ('grp', 'dp'), scatter_dimension=0, tiled=True)  216 us
    all_gather x1, waiting for transfers between devices, on_device(): lax.all_gather(qkv_weight, ('grp', 'dp'), axis=2, tiled=True)  156 us
    all_gather x2, waiting for transfers between devices, on_device(): whole = lax.all_gather(state, 'seq', axis=1, tiled=True)  134 us
    all_gather x1, waiting for transfers between devices, on_device(): lax.all_gather(out_weight, ('grp', 'dp'), axis=0, tiled=True)  125 us
    all_gather x2, waiting for transfers between devices, on_device(): attn_all = lax.all_gather(attn, 'seq', axis=1, tiled=True)  88.4 us
  transfers between devices with their start and end apart: 7, of which 7 were waited for; matrix products, arithmetic and copies ran while one was open for 3% of the time, Pallas kernels for 0%

commit v1 on v0

--- a/solution.py
+++ b/solution.py
@@ -10,6 +10,16 @@
 CLIP_RANGE = 0.2
 REWARD_FLOOR = 0.75
 NORM_EPS = 1e-06
+
+
+def obtain_words_on(base_x):
+    block_now = jnp.concatenate(
+        lax.all_to_all(
+            jnp.stack([base_x for _ in range(lax.axis_size(("grp", "dp")))]), ("grp", "dp"), 0, 0
+        ),
+        axis=2,
+    )
+    return block_now
 
 
 def advantages(rewards, group_ids):
@@ -41,7 +51,7 @@
     log_ratio,
 ):
     qkv_full, out_rows = (
-        lax.all_gather(qkv_weight, ("grp", "dp"), axis=2, tiled=True),
+        obtain_words_on(qkv_weight),
         lax.all_gather(out_weight, ("grp", "dp"), axis=0, tiled=True),
     )
     group_width = qkv_full.shape[1]

time: 782 us -> 691 us (0.88)
  waiting for transfers between devices: 721 us -> 614 us
  starting transfers between devices: 0.28 us -> 19.3 us
    all_gather x1 -> x0, waiting for transfers between devices: 156 us -> none  [on_device(): lax.all_gather(qkv_weight, ('grp', 'dp'), axis=2, tiled=True)]
    all_to_all x0 -> x1, waiting for transfers between devices: none -> 92.5 us  [obtain_words_on(): lax.all_to_all(jnp.stack([base_x for _ in range(lax.axis_size(('grp', 'dp...]
    all_gather x1, waiting for transfers between devices: 125 us -> 69.1 us  [on_device(): lax.all_gather(out_weight, ('grp', 'dp'), axis=0, tiled=True)]
    all_to_all x0 -> x1, starting transfers between devices: none -> 18.9 us  [obtain_words_on(): lax.all_to_all(jnp.stack([base_x for _ in range(lax.axis_size(('grp', 'dp...]
    all_gather x2, waiting for transfers between devices: 134 us -> 147 us  [on_device(): whole = lax.all_gather(state, 'seq', axis=1, tiled=True)]
    all_gather x1 -> x0, local copies, waits for them, and re-layouts: 8.55 us -> none  [on_device(): lax.all_gather(qkv_weight, ('grp', 'dp'), axis=2, tiled=True)]
  transfers between devices with their start and end apart: 7 -> 7, of which waited for: 7 -> 7; matrix products, arithmetic and copies ran while one was open for 3% -> 2% of each run, Pallas kernels for 0% -> 0%
where the time goes in v1:
time: 691 us; the launch traced here: 690 us
  waiting for transfers between devices  614 us (89%)
  starting transfers between devices  19.3 us (3%)
  matrix products  19.3 us (3%)
  between operations  18.6 us (3%)
  local copies, waits for them, and re-layouts  12.1 us (2%)
    reduce_scatter x1, waiting for transfers between devices, on_device(): lax.psum_scatter(gradient, ('grp', 'dp'), scatter_dimension=0, tiled=True)  216 us
    all_gather x2, waiting for transfers between devices, on_device(): whole = lax.all_gather(state, 'seq', axis=1, tiled=True)  147 us
    all_to_all x1, waiting for transfers between devices, obtain_words_on(): lax.all_to_all(jnp.stack([base_x for _ in range(lax.axis_size(('grp', 'dp...  92.5 us
    all_gather x2, waiting for transfers between devices, on_device(): attn_all = lax.all_gather(attn, 'seq', axis=1, tiled=True)  88.5 us
    all_gather x1, waiting for transfers between devices, on_device(): lax.all_gather(out_weight, ('grp', 'dp'), axis=0, tiled=True)  69.1 us
    all_to_all x1, starting transfers between devices, obtain_words_on(): lax.all_to_all(jnp.stack([base_x for _ in range(lax.axis_size(('grp', 'dp...  18.9 us
  transfers between devices with their start and end apart: 7, of which 7 were waited for; matrix products, arithmetic and copies ran while one was open for 2% of the time, Pallas kernels for 0%

profile of v1, /device:TPU:8, one launch (start us, length us, event | category | flops | bytes accessed | tf_op | source)
XLA Modules:
  0.0 690.1 jit_solution(9904969713829516201)
XLA Ops:
  7.2 3.0 stack.10
  10.1 18.9 %all-to-all-start = ((bf16[64,3,256,38]{2,3,1,0:T(8,128)(2,1)}), bf16[64,3,256,38]{2,3,1,0:T(8,128)(2,1)}, u32[]{:S(2)}, u32[]{:S(2)}) async-start(bf16[64,3,256,38]{2,3,1,0:T(8,128)(2,1)} %stack.10), calls=%async_computation | async-start | bytes 7864320 | tf_op jit(solution)/shard_map/all_to_all | solution.py:17
  29.1 0.0 all-gather.15.cloned.1.call-start
  29.1 0.7 all-gather.15.cloned.1.call-update
  29.9 0.7 all-gather.9.cloned.1.call-update
  30.6 0.0 all-gather.7.cloned.1.call-start
  31.3 0.2 multiply_reduce_fusion.2
  31.5 0.1 fusion.35
  31.6 80.7 %all-gather.15.cloned.1.call-done = f32[1,256,2432]{1,2,0:T(8,128)} async-done(((f32[1,256,304]{1,2,0:T(8,128)}), f32[1,256,2432]{1,2,0:T(8,128)}) %all-gather.15.cloned.1.call-update) | async-done | bytes 2490384 | tf_op jit(solution)/shard_map/all_gather | solution.py:79
  112.3 2.2 reduce_sum.108
  114.4 0.3 copy-done
  114.7 0.4 multiply_reduce_fusion.1
  115.1 92.5 %all-to-all-done = bf16[64,3,256,38]{2,3,1,0:T(8,128)(2,1)} async-done(((bf16[64,3,256,38]{2,3,1,0:T(8,128)(2,1)}), bf16[64,3,256,38]{2,3,1,0:T(8,128)(2,1)}, u32[]{:S(2)}, u32[]{:S(2)}) %all-to-all-start) | async-done | bytes 3735584 | tf_op jit(solution)/shard_map/all_to_all | solution.py:17
  207.6 4.0 copy.31
  211.6 1.1 copy.38
  212.7 1.8 copy-done.2
  214.5 1.8 convolution_convert_fusion.1
  216.3 0.2 copy.32
  216.5 0.5 fusion.44
  217.0 0.3 convolution_multiply_fusion.1
  217.4 1.0 convolution_convert_fusion.3
  218.5 0.0 all-gather.11.cloned.1.call-start
  218.7 69.1 %all-gather.9.cloned.1.call-done = bf16[2048,304]{1,0:T(8,128)(2,1)} async-done(((bf16[32,304]{1,0:T(8,128)(2,1)}), bf16[2048,304]{1,0:T(8,128)(2,1)}) %all-gather.9.cloned.1.call-update) | async-done | bytes 1245200 | tf_op jit(solution)/shard_map/all_gather | solution.py:55
  287.7 43.9 %all-gather.7.cloned.1.call-done = bf16[256,2048]{0,1:T(8,128)(2,1)} async-done(((bf16[256,256]{0,1:T(8,128)(2,1)}), bf16[256,2048]{0,1:T(8,128)(2,1)}) %all-gather.7.cloned.1.call-update) | async-done | bytes 1048592 | tf_op jit(solution)/shard_map/all_gather | solution.py:103
  331.6 3.1 fusion.18
  334.8 0.2 all-gather.13.cloned.1.call-start
  335.0 0.1 fusion.34
  335.0 66.2 %all-gather.11.cloned.1.call-done = f32[256,2432]{0,1:T(8,128)} async-done(((f32[256,304]{0,1:T(8,128)}), f32[256,2432]{0,1:T(8,128)}) %all-gather.11.cloned.1.call-update) | async-done | bytes 2490384 | tf_op jit(solution)/shard_map/all_gather | solution.py:79
  401.2 2.2 reduce_sum.112
  403.4 0.3 copy-done.1
  403.7 0.4 multiply_reduce_fusion
  404.0 3.8 convolution_convert_fusion
  407.8 0.2 copy.34
  408.0 0.5 fusion.45
  408.5 0.3 convolution_multiply_fusion
  408.9 1.0 convolution_convert_fusion.2
  410.0 0.0 reduce-scatter.2.cloned.1.call-start
  410.2 0.2 fusion.32
  410.4 0.2 fusion.33
  410.6 0.7 fusion.37
  411.3 0.6 fusion.43
  413.3 0.1 fusion.31
  413.3 44.7 %all-gather.13.cloned.1.call-done = bf16[256,2048]{0,1:T(8,128)(2,1)} async-done(((bf16[256,256]{0,1:T(8,128)(2,1)}), bf16[256,2048]{0,1:T(8,128)(2,1)}) %all-gather.13.cloned.1.call-update) | async-done | bytes 1048592 | tf_op jit(solution)/shard_map/all_gather | solution.py:103
  458.0 4.2 convolution_bitcast_fusion
  463.0 0.1 copy-done.5
  463.1 0.6 copy-done.10
  463.7 2.6 fusion.22
  466.3 215.8 %reduce-scatter.2.cloned.1.call-done = f32[32,304]{1,0:T(8,128)} async-done(((f32[2048,304]{1,0:T(8,128)}), f32[32,304]{1,0:T(8,128)}) %reduce-scatter.2.cloned.1.call-update) | async-done | bytes 38928 | tf_op jit(solution)/shard_map/reduce_scatter | solution.py:124
  (32 shorter events, 0.2 us)
Async XLA Ops:
  10.1 21.1 %copy-start.6 = (f32[10,2,2432]{2,1,0:T(2,128)S(1)}, f32[10,2,2432]{2,1,0:T(2,128)}, u32[]{:S(2)}) copy-start(f32[10,2,2432]{2,1,0:T(2,128)} %param.11) | copy-start | bytes 583684
  10.1 197.4 %all-to-all-start = ((bf16[64,3,256,38]{2,3,1,0:T(8,128)(2,1)}), bf16[64,3,256,38]{2,3,1,0:T(8,128)(2,1)}, u32[]{:S(2)}, u32[]{:S(2)}) async-start(bf16[64,3,256,38]{2,3,1,0:T(8,128)(2,1)} %stack.10), calls=%async_computation | async-start | bytes 7864320 | tf_op jit(solution)/shard_map/all_to_all | solution.py:17
  29.1 83.2 %all-gather.15.cloned.1.call-start = ((), (), s32[]{:S(2)}) async-start(), calls=%async_computation.7 | async-start | bytes 2801664 | tf_op jit(solution)/shard_map/all_gather | solution.py:79
  29.8 257.9 %all-gather.9.cloned.1.call-start = ((), (), s32[]{:S(2)}) async-start(), calls=%async_computation.3 | async-start | bytes 1597440 | tf_op jit(solution)/shard_map/all_gather | solution.py:55
  30.6 301.0 %all-gather.7.cloned.1.call-start = ((), (), s32[]{:S(2)}) async-start(), calls=%async_computation.2 | async-start | bytes 1179648 | tf_op jit(solution)/shard_map/all_gather | solution.py:103
  112.3 2.5 copy-start
  212.7 1.8 copy-start.2
  217.4 114.2 %copy-start.3 = (f32[1,256,304]{1,2,0:T(8,128)S(1)}, f32[1,256,304]{1,2,0:T(8,128)}, u32[]{:S(2)}) copy-start(f32[1,256,304]{1,2,0:T(8,128)} %param.9) | copy-start | bytes 933892
  217.4 114.2 %copy-start.4 = (bf16[2,1,256,304]{2,3,1,0:T(8,128)(2,1)S(1)}, bf16[2,1,256,304]{2,3,1,0:T(8,128)(2,1)}, u32[]{:S(2)}) copy-start(bf16[2,1,256,304]{2,3,1,0:T(8,128)(2,1)} %param.10) | copy-start | bytes 933892
  218.5 182.7 %all-gather.11.cloned.1.call-start = ((), (), s32[]{:S(2)}) async-start(), calls=%async_computation.4 | async-start | bytes 2801664 | tf_op jit(solution)/shard_map/all_gather | solution.py:79
  334.8 123.2 %all-gather.13.cloned.1.call-start = ((), (), s32[]{:S(2)}) async-start(), calls=%async_computation.5 | async-start | bytes 1179648 | tf_op jit(solution)/shard_map/all_gather | solution.py:103
  401.2 2.5 copy-start.1
  408.9 1.3 copy-start.7
  408.9 1.3 copy-start.8
  408.9 1.7 copy-start.9
  408.9 49.1 %copy-start.11 = (bf16[256,2048]{0,1:T(8,128)(2,1)S(1)}, bf16[256,2048]{0,1:T(8,128)(2,1)}, u32[]{:S(2)}) copy-start(bf16[256,2048]{0,1:T(8,128)(2,1)} %all-gather.7.cloned.1.call-done) | copy-start | bytes 3145732
  410.0 272.1 %reduce-scatter.2.cloned.1.call-start = ((), (), s32[]{:S(2)}) async-start(), calls=%async_computation.6 | async-start | bytes 3194880 | tf_op jit(solution)/shard_map/reduce_scatter | solution.py:124
  462.1 1.0 copy-start.5
  462.2 1.5 copy-start.10
Sparse Core Ops, SparseCore 0:
  32.0 80.2 all-gather.14
  115.5 172.1 all-gather.8
  290.4 41.1 all-gather.6
  334.9 66.2 all-gather.10
  410.1 47.8 all-gather.12
  463.1 218.9 reduce-scatter.1
